TPU v7x, 256 devices: a whole 4x4x8 slice. The times are simulated.
256 devices in a mesh: seq: 8 (over z_lo, core), blk: 32 (over y, z_hi, x).
Axes of the slice: x: 4, y: 4, z: 8 (z_hi: 2, z_lo: 4; z = z_hi * 4 + z_lo), core: 2. Of those that a mesh axis runs over, the one named last changes fastest.
Arguments:
- stream: float32 [4096, 3072], P(('seq', 'blk')), may hold values from -39 to 39
- key_keep: int32 [4096], replicated, may hold values 0 or 1
- positions: int32 [4096, 3], replicated, may hold values from 0 to 63
- lengths: int32 [4], replicated, may hold values from 1 to 2048, 4096 in all
- step_index: int32 [4], replicated, may hold values from 0 to 27
- mod_table: bfloat16 [4, 28, 3, 3072], replicated, may hold values from -4 to 4
- w_qkv: bfloat16 [3072, 9216], P(None, 'blk'), may hold values from -0.109375 to 0.109375
- w_mlp_in: bfloat16 [3072, 12288], P(None, 'blk'), may hold values from -0.109375 to 0.109375
- q_gain: float32 [128], replicated, may hold values from 0.5 to 10
- k_gain: float32 [128], replicated, may hold values from 0.5 to 10
- w_attn_out: bfloat16 [3072, 3072], P('blk'), may hold values from -0.109375 to 0.109375
- w_mlp_out: bfloat16 [12288, 3072], P('blk'), may hold values from -0.0546875 to 0.0546875
Outputs:
- stream_next: float32 [4096, 3072], P(('seq', 'blk'))
Inputs may be any that keep to these rules, and one draw needn't show every extreme that they name: The lengths sum to 4096; the longest request has exactly 2048 tokens.
All inputs are finite; a program needn't handle non-finite values.
Results may differ from a plain program's by a relative error of at most 0.0082.
The roundings to bfloat16 on the way count: a program that leaves them out, or rounds other values in their place, can miss the bound.
Values may be sent and summed in bfloat16 or wider, within the bound.
No kernel may reach another device: no remote copies, remote signals or barrier semaphores. Data moves between devices by JAX's collectives and lax.ppermute only.
A program may use at most 64 MiB of HBM per device.

v0:
```python
import math
import jax
import jax.numpy as jnp
from jax import lax
from jax.sharding import PartitionSpec as P


def rope_table(head_size):
    first_count = head_size // 16
    second = 7 * head_size // 32
    pair_ids = jnp.arange(head_size // 2, dtype=jnp.int32)
    pair_axis = jnp.where(
        pair_ids < first_count, 0, jnp.where(pair_ids < first_count + second, 1, 2)
    )
    pair_local = jnp.where(
        pair_ids < first_count,
        pair_ids,
        jnp.where(
            pair_ids < first_count + second, pair_ids - first_count, pair_ids - first_count - second
        ),
    )
    axis_dims = jnp.where(pair_axis == 0, 2 * first_count, 2 * second)
    frequency = jnp.power(
        jnp.float32(10000.0), -(2 * pair_local).astype(jnp.float32) / axis_dims.astype(jnp.float32)
    )
    return jnp.where(
        jnp.arange(3)[:, None] == pair_axis[None, :], frequency[None, :], jnp.float32(0.0)
    )


def angles_of(places, freq_table):
    return jnp.sum(places.astype(jnp.float32)[:, :, None] * freq_table[None, :, :], axis=1)


def rotate(values, angles):
    paired = values.reshape(values.shape[:-1] + (values.shape[-1] // 2, 2))
    even_part = paired[..., 0]
    odd_part = paired[..., 1]
    cos_part = jnp.cos(angles)[:, None, :]
    sin_part = jnp.sin(angles)[:, None, :]
    turned = jnp.stack(
        [cos_part * even_part - sin_part * odd_part, sin_part * even_part + cos_part * odd_part],
        axis=-1,
    )
    return turned.reshape(values.shape)


def rms_scale(values, gain_vec):
    return values * lax.rsqrt(jnp.mean(values * values, axis=-1, keepdims=True) + 1e-06) * gain_vec


def segment_of(row_ids, request_ends):
    return jnp.sum((row_ids[:, None] >= request_ends[None, :]).astype(jnp.int32), axis=1)


def spread_rows(row_ids, query_rows, block_rows, tok_seq):
    owner = row_ids // query_rows
    within = row_ids % query_rows
    return within // block_rows * tok_seq + owner * block_rows + within % block_rows


def body(
    stream,
    key_keep,
    positions,
    lengths,
    step_index,
    mod_table,
    w_qkv,
    w_mlp_in,
    q_gain,
    k_gain,
    w_attn_out,
    w_mlp_out,
):
    blk_count = lax.axis_size("blk")
    seq_count = lax.axis_size("seq")
    seq_at = lax.axis_index("seq")
    blk_at = lax.axis_index("blk")
    block_rows = stream.shape[0]
    width = stream.shape[1]
    tok_seq = block_rows * blk_count
    head_size = q_gain.shape[0]
    local_heads = width // head_size // seq_count
    requests = mod_table.shape[0]
    step_total = mod_table.shape[1]
    inv_root = 1.0 / math.sqrt(head_size)
    request_ends = jnp.cumsum(lengths)
    own_rows = seq_at * tok_seq + blk_at * block_rows + jnp.arange(block_rows, dtype=jnp.int32)
    own_request = segment_of(own_rows, request_ends)
    step_pick = (jnp.arange(step_total, dtype=jnp.int32)[None, :] == step_index[:, None]).astype(
        jnp.bfloat16
    )
    modulation = jnp.einsum(
        "rs,rsk->rk",
        step_pick,
        mod_table.reshape(requests, step_total, 3 * width),
        preferred_element_type=jnp.float32,
    )
    member = (own_request[:, None] == jnp.arange(requests, dtype=jnp.int32)[None, :]).astype(
        jnp.float32
    )
    token_mod = jnp.dot(member, modulation, precision=lax.Precision.HIGHEST)
    mod_shift = token_mod[:, :width]
    mod_scale = token_mod[:, width : 2 * width]
    mod_gate = token_mod[:, 2 * width :]
    row_mean = jnp.mean(stream, axis=1, keepdims=True)
    centered = stream - row_mean
    row_var = jnp.mean(centered * centered, axis=1, keepdims=True)
    normed = centered * lax.rsqrt(row_var + 1e-06)
    modin = ((1.0 + mod_scale) * normed + mod_shift).astype(jnp.bfloat16)
    qkv_width = w_qkv.shape[1]
    shard_rows = lax.all_to_all(
        jnp.broadcast_to(modin[None], (blk_count,) + modin.shape), "blk", 0, 0, tiled=True
    ).reshape(blk_count * block_rows, width)
    qkv_part = jnp.dot(shard_rows, w_qkv, preferred_element_type=jnp.float32).astype(jnp.bfloat16)
    mlp_part = jax.nn.gelu(
        jnp.dot(shard_rows, w_mlp_in, preferred_element_type=jnp.float32), approximate=True
    ).astype(jnp.bfloat16)
    joined = jnp.concatenate([qkv_part, mlp_part], axis=1)
    qkv_cols = joined[:, :qkv_width]
    mlp_act = joined[:, qkv_width:]
    heads_in = lax.all_to_all(
        lax.all_to_all(qkv_cols, "blk", split_axis=0, concat_axis=1, tiled=True),
        "seq",
        split_axis=1,
        concat_axis=0,
        tiled=True,
    )
    query_rows = heads_in.shape[0]
    heads4 = heads_in.reshape(query_rows, local_heads, 3, head_size)
    query_ids = spread_rows(
        blk_at * query_rows + jnp.arange(query_rows, dtype=jnp.int32),
        query_rows,
        block_rows,
        tok_seq,
    )
    query_request = segment_of(query_ids, request_ends)
    angles = angles_of(jnp.take(positions, query_ids, axis=0), rope_table(head_size))
    query_rot = rotate(rms_scale(heads4[:, :, 0].astype(jnp.float32), q_gain), angles).astype(
        jnp.bfloat16
    )
    key_rot = rotate(rms_scale(heads4[:, :, 1].astype(jnp.float32), k_gain), angles).astype(
        jnp.bfloat16
    )
    value_rows = heads4[:, :, 2]
    run_top = jnp.full((query_rows, local_heads), -1e30, jnp.float32)
    key_part = lax.all_gather(key_rot, "blk", axis=0, tiled=True)
    value_part = lax.all_gather(value_rows, "blk", axis=0, tiled=True)
    key_ids = spread_rows(
        jnp.arange(key_part.shape[0], dtype=jnp.int32), query_rows, block_rows, tok_seq
    )
    key_request = segment_of(key_ids, request_ends)
    kept = jnp.take(key_keep, key_ids) == 1
    visible = (
        (query_request[:, None] == key_request[None, :])
        & (kept[None, :] | (query_ids[:, None] == key_ids[None, :]))
    )[:, None, :]
    scores = (
        jnp.einsum("qhd,khd->qhk", query_rot, key_part, preferred_element_type=jnp.float32)
        * inv_root
    )
    row_high = jnp.max(jnp.where(visible, scores, -1e30), axis=2)
    new_top = jnp.maximum(run_top, row_high)
    weights = jnp.where(visible, jnp.exp(scores - new_top[:, :, None]), 0.0)
    run_norm = jnp.sum(weights, axis=2)
    run_sum = jnp.einsum(
        "qhk,khd->qhd", weights.astype(jnp.bfloat16), value_part, preferred_element_type=jnp.float32
    )
    run_top, run_norm, run_sum = (new_top, run_norm, run_sum)
    attended = (run_sum / run_norm[:, :, None]).astype(jnp.bfloat16)
    attended = attended.reshape(query_rows, local_heads * head_size)
    attn_local = lax.all_to_all(
        lax.all_to_all(attended, "seq", split_axis=0, concat_axis=1, tiled=True),
        "blk",
        split_axis=1,
        concat_axis=0,
        tiled=True,
    )
    mlp_part = mlp_act
    partial = (
        jnp.dot(attn_local, w_attn_out, preferred_element_type=jnp.float32)
        + jnp.dot(mlp_part, w_mlp_out, preferred_element_type=jnp.float32)
    ).astype(jnp.bfloat16)
    pieces = lax.all_to_all(partial.reshape(blk_count, block_rows, width), "blk", 0, 0, tiled=True)
    summed = jnp.sum(pieces.astype(jnp.float32), axis=0)
    return stream + mod_gate * summed


def solution(mesh):
    in_specs = (
        P(("seq", "blk"), None),
        P(),
        P(),
        P(),
        P(),
        P(),
        P(None, "blk"),
        P(None, "blk"),
        P(),
        P(),
        P("blk", None),
        P("blk", None),
    )
    out_specs = P(("seq", "blk"), None)
    return jax.shard_map(body, mesh=mesh, in_specs=in_specs, out_specs=out_specs, check_vma=False)
```

profile of v0, /device:TPU:2, one launch (start us, length us, event | category | flops | bytes accessed | tf_op | source)
XLA Modules:
  0.0 507.3 jit_solution(7781617142355008761)
XLA Ops:
  6.5 0.9 fusion.70
  7.4 1.1 reduce_sum.91
  8.5 1.1 multiply_reduce_fusion.2
  9.6 0.8 reduce-window.8
  10.6 2.8 fusion.11
  13.4 0.4 fusion.44
  13.8 0.1 fusion.41
  14.0 2.0 broadcast_in_dim.66
  16.0 14.3 %all-to-all-start = ((bf16[32,16,3072]{2,1,0:T(8,128)(2,1)}), bf16[32,16,3072]{2,1,0:T(8,128)(2,1)}, u32[]{:S(2)}, u32[]{:S(2)}) async-start(bf16[32,16,3072]{2,1,0:T(8,128)(2,1)} %broadcast_in_dim.66), calls=%async_computation | async-start | bytes 6291456 | tf_op jit(solution)/shard_map/all_to_all | solution.py:113
  30.3 73.6 %all-to-all-done = bf16[32,16,3072]{2,1,0:T(8,128)(2,1)} async-done(((bf16[32,16,3072]{2,1,0:T(8,128)(2,1)}), bf16[32,16,3072]{2,1,0:T(8,128)(2,1)}, u32[]{:S(2)}, u32[]{:S(2)}) %all-to-all-start) | async-done | bytes 3145760 | tf_op jit(solution)/shard_map/all_to_all | solution.py:113
  104.0 3.6 convolution_convert_fusion
  107.5 0.9 copy.79
  108.5 7.2 %all-to-all-start.1 = ((bf16[32,16,288]{2,1,0:T(8,128)(2,1)}), bf16[32,16,288]{2,1,0:T(8,128)(2,1)S(1)}, u32[]{:S(2)}, u32[]{:S(2)}) async-start(bf16[32,16,288]{2,1,0:T(8,128)(2,1)} %bitcast.71), calls=%async_computation.1 | async-start | bytes 786432 | tf_op jit(solution)/shard_map/all_to_all | solution.py:124
  115.7 0.7 mul.314
  116.5 0.7 mul.325
  117.2 2.8 copy.83
  120.0 2.8 gather_fusion.1
  122.9 0.9 copy.84
  123.8 0.5 fusion.78
  124.4 4.0 all-to-all-done.1
  128.4 0.8 copy.80
  129.2 1.5 all_to_all.60
  130.6 0.7 copy.81
  131.4 5.7 %all-to-all-start.2 = ((bf16[16,8,1152]{2,0,1:T(8,128)(2,1)}), bf16[16,8,1152]{2,0,1:T(8,128)(2,1)S(1)}, u32[]{:S(2)}, u32[]{:S(2)}) async-start(bf16[16,8,1152]{2,0,1:T(8,128)(2,1)} %copy.81), calls=%async_computation.2 | async-start | bytes 589824 | tf_op jit(solution)/shard_map/all_to_all | solution.py:123
  137.2 0.7 fusion.71
  137.8 0.1 multiply_reduce_fusion.3
  137.9 0.8 fusion.87
  138.7 8.9 %all-to-all-done.2 = bf16[16,8,1152]{2,0,1:T(8,128)(2,1)S(1)} async-done(((bf16[16,8,1152]{2,0,1:T(8,128)(2,1)}), bf16[16,8,1152]{2,0,1:T(8,128)(2,1)S(1)}, u32[]{:S(2)}, u32[]{:S(2)}) %all-to-all-start.2) | async-done | bytes 294944 | tf_op jit(solution)/shard_map/all_to_all | solution.py:123
  147.5 0.7 copy-done.5
  148.2 1.1 reshape.627
  149.3 1.1 fusion.86
  150.4 0.7 multiply_reduce_fusion
  151.1 0.7 copy_convert_fusion
  151.8 0.6 add_rsqrt_fusion.1
  152.4 1.7 copy.86
  154.1 1.3 add_rsqrt_fusion
  155.4 0.8 copy.91
  156.2 1.1 multiply_multiply_fusion.2
  157.3 1.1 multiply_multiply_fusion.1
  158.4 2.0 subtract_convert_fusion
  160.4 0.2 pad_maximum_fusion
  160.6 0.7 copy.89
  161.4 0.2 all-gather.6.cloned.1.call-start
  161.6 0.8 copy.106
  162.4 0.1 compare_select_fusion
  162.6 23.0 %gather_fusion = s32[4096]{0:T(1024)S(1)} fusion(s32[4096]{0:T(1024)S(1)} %copy-done.1, s32[4096]{0:T(1024)S(1)} %broadcast_clamp_fusion), kind=kCustom, calls=%fused_computation | custom fusion | bytes 49152 | tf_op jit(solution)/shard_map/jit(_take)/gather | solution.py:154
  185.7 0.1 convert_reduce_fusion.1
  185.9 4.5 or_and_fusion
  190.4 0.2 pad_maximum_fusion.1
  190.7 67.6 %all-gather.4.cloned.1.call-done = bf16[4096,3,128]{2,0,1:T(8,128)(2,1)} async-done(((bf16[128,3,128]{2,0,1:T(8,128)(2,1)}), bf16[4096,3,128]{2,0,1:T(8,128)(2,1)}) %all-gather.4.cloned.1.call-update) | async-done | bytes 3145744 | tf_op jit(solution)/shard_map/all_gather | solution.py:148
  258.3 3.2 fusion
  261.5 2.6 copy-done.2
  264.1 1.2 fusion.3
  265.3 106.2 %all-gather.6.cloned.1.call-done = bf16[4096,3,1,128]{0,3,1,2:T(8,128)(2,1)} async-done(((bf16[128,3,1,128]{0,3,1,2:T(8,128)(2,1)}), bf16[4096,3,1,128]{0,3,1,2:T(8,128)(2,1)}) %all-gather.6.cloned.1.call-update) | async-done | bytes 3145744 | tf_op jit(solution)/shard_map/all_gather | solution.py:149
  371.5 5.3 %fusion.23 = bf16[128,3,128]{0,2,1:T(8,128)(2,1)S(1)} fusion(f32[3,4096,128]{2,1,0:T(8,128)} %copy-done.2, f32[128,3]{0,1:T(4,128)S(1)} %broadcast_maximum_fusion, pred[128,4096]{0,1:T(8,128)(4,1)} %or_and_fusion, bf16[4096,3,1,128]{0,3,1,2:T(8,128)(2,1)} %all-gather.6.cloned.1.call-done, f32[128,3]{0,1:T(4,128)S(1)} %fusion.3), kind=kOutput, calls=%fused_computation.24 | convolution fusion | flops 407470080 | bytes 10062848 | tf_op jit(solution)/shard_map/qhk,khd->qhd/dot_general | solution.py:167
  376.9 0.1 copy.96
  377.1 8.7 %all_to_all.77 = bf16[8,16,384]{2,1,0:T(8,128)(2,1)S(1)} all-to-all(bf16[8,16,384]{2,1,0:T(8,128)(2,1)S(1)} %all_to_all.63), channel_id=1, replica_groups=mesh['seq'=8,'blk'=32] {'seq'}, dimensions={0} | all-to-all | bytes 196608 | tf_op jit(solution)/shard_map/all_to_all | solution.py:174
  385.8 0.1 all_to_all.66
  386.0 19.6 %all_to_all.78 = bf16[16,32,96]{2,0,1:T(8,128)(2,1)S(1)} all-to-all(bf16[16,32,96]{2,0,1:T(8,128)(2,1)S(1)} %copy.98), channel_id=1, replica_groups=mesh['seq'=8,'blk'=32] {'blk'}, dimensions={1} | all-to-all | bytes 196608 | tf_op jit(solution)/shard_map/all_to_all | solution.py:173
  405.6 4.7 fusion.90
  410.3 9.6 %add_convert_fusion = bf16[512,3072]{1,0:T(8,128)(2,1)} fusion(f32[512,3072]{1,0:T(8,128)} %fusion.90, bf16[384,3072]{1,0:T(8,128)(2,1)S(1)} %copy-done, bf16[512,3072]{1,0:T(8,128)(2,1)} %bitcast.5, bf16[3072,384]{1,0:T(8,128)(2,1)} %param.19), kind=kOutput, calls=%fused_computation.8 | convolution fusion | flops 2420834304 | bytes 17301504 | tf_op jit(solution)/shard_map/dot_general | solution.py:183
  419.9 79.4 %all_to_all.79 = bf16[32,16,3072]{2,1,0:T(8,128)(2,1)S(1)} all-to-all(bf16[32,16,3072]{2,1,0:T(8,128)(2,1)} %bitcast.68), channel_id=1, replica_groups=mesh['seq'=8,'blk'=32] {'blk'}, dimensions={0} | all-to-all | bytes 6291456 | tf_op jit(solution)/shard_map/all_to_all | solution.py:185
  499.3 0.5 convert_reduce_fusion
  499.8 0.7 fusion.43
  (45 shorter events, 0.6 us)
Async XLA Ops:
  6.5 403.8 %copy-start = (bf16[384,3072]{1,0:T(8,128)(2,1)S(1)}, bf16[384,3072]{1,0:T(8,128)(2,1)}, u32[]{:S(2)}) copy-start(bf16[384,3072]{1,0:T(8,128)(2,1)} %param.23) | copy-start | bytes 7077892
  6.5 7.3 %copy-start.3 = (f32[16,3072]{1,0:T(8,128)S(1)}, f32[16,3072]{1,0:T(8,128)}, u32[]{:S(2)}) copy-start(f32[16,3072]{1,0:T(8,128)} %param.12) | copy-start | bytes 589828
  10.5 5.5 %copy-start.11 = (s32[4,1]{0,1:T(1,128)}, s32[4,1]{0,1:T(1,128)S(1)}, u32[]{:S(2)}) copy-start(s32[4,1]{0,1:T(1,128)S(1)} %reduce-window.8) | copy-start | bytes 52
  16.0 87.9 %all-to-all-start = ((bf16[32,16,3072]{2,1,0:T(8,128)(2,1)}), bf16[32,16,3072]{2,1,0:T(8,128)(2,1)}, u32[]{:S(2)}, u32[]{:S(2)}) async-start(bf16[32,16,3072]{2,1,0:T(8,128)(2,1)} %broadcast_in_dim.66), calls=%async_computation | async-start | bytes 6291456 | tf_op jit(solution)/shard_map/all_to_all | solution.py:113
  103.9 11.8 %copy-start.9 = (f32[128]{0:T(128)S(1)}, f32[128]{0:T(128)}, u32[]{:S(2)}) copy-start(f32[128]{0:T(128)} %param.21) | copy-start | bytes 1540
  104.0 12.5 %copy-start.10 = (f32[128]{0:T(128)S(1)}, f32[128]{0:T(128)}, u32[]{:S(2)}) copy-start(f32[128]{0:T(128)} %param.20) | copy-start | bytes 1540
  108.5 19.9 %all-to-all-start.1 = ((bf16[32,16,288]{2,1,0:T(8,128)(2,1)}), bf16[32,16,288]{2,1,0:T(8,128)(2,1)S(1)}, u32[]{:S(2)}, u32[]{:S(2)}) async-start(bf16[32,16,288]{2,1,0:T(8,128)(2,1)} %bitcast.71), calls=%async_computation.1 | async-start | bytes 786432 | tf_op jit(solution)/shard_map/all_to_all | solution.py:124
  131.4 16.2 %all-to-all-start.2 = ((bf16[16,8,1152]{2,0,1:T(8,128)(2,1)}), bf16[16,8,1152]{2,0,1:T(8,128)(2,1)S(1)}, u32[]{:S(2)}, u32[]{:S(2)}) async-start(bf16[16,8,1152]{2,0,1:T(8,128)(2,1)} %copy.81), calls=%async_computation.2 | async-start | bytes 589824 | tf_op jit(solution)/shard_map/all_to_all | solution.py:123
  137.1 121.1 %all-gather.4.cloned.1.call-start = ((), (), s32[]{:S(2)}) async-start(), calls=%async_computation.6 | async-start | bytes 3244032 | tf_op jit(solution)/shard_map/all_gather | solution.py:148
  147.5 0.7 copy-start.5
  148.2 14.3 %copy-start.1 = (s32[4096]{0:T(1024)S(1)}, s32[4096]{0:T(1024)}, u32[]{:S(2)}) copy-start(s32[4096]{0:T(1024)} %param.13) | copy-start | bytes 49156
  150.4 11.2 %copy-start.6 = (bf16[128,3,1,128]{3,2,1,0:T(2,128)(2,1)S(1)}, bf16[128,3,1,128]{3,2,1,0:T(2,128)(2,1)}, u32[]{:S(2)}) copy-start(bf16[128,3,1,128]{3,2,1,0:T(2,128)(2,1)} %get-tuple-element.5) | copy-start | bytes 294916
  161.4 210.2 %all-gather.6.cloned.1.call-start = ((), (), s32[]{:S(2)}) async-start(), calls=%async_computation.7 | async-start | bytes 3244032 | tf_op jit(solution)/shard_map/all_gather | solution.py:149
  162.5 23.1 %copy-start.12 = (s32[4,1]{0,1:T(1,128)S(1)}, s32[4,1]{0,1:T(1,128)}, u32[]{:S(2)}) copy-start(s32[4,1]{0,1:T(1,128)} %copy-done.11) | copy-start | bytes 52
  162.5 27.9 %copy-start.7 = (bf16[128,3,64,1]{0,3,2,1:T(2,128)(2,1)S(1)}, bf16[128,3,64,1]{0,3,2,1:T(2,128)(2,1)}, u32[]{:S(2)}) copy-start(bf16[128,3,64,1]{0,3,2,1:T(2,128)(2,1)} %get-tuple-element.8) | copy-start | bytes 147460
  162.5 27.9 %copy-start.8 = (bf16[128,3,64,1]{0,3,2,1:T(2,128)(2,1)S(1)}, bf16[128,3,64,1]{0,3,2,1:T(2,128)(2,1)}, u32[]{:S(2)}) copy-start(bf16[128,3,64,1]{0,3,2,1:T(2,128)(2,1)} %get-tuple-element.9) | copy-start | bytes 147460
  258.3 5.9 %copy-start.4 = (pred[128,4096]{0,1:T(8,128)(4,1)S(1)}, pred[128,4096]{0,1:T(8,128)(4,1)}, u32[]{:S(2)}) copy-start(pred[128,4096]{0,1:T(8,128)(4,1)} %or_and_fusion) | copy-start | bytes 1572868
  261.4 2.7 copy-start.2
Sparse Core Ops, SparseCore 0:
  161.5 96.7 all-gather.3
  261.5 110.0 all-gather.5
where the time goes:
time: 508 us; the launch traced here: 507 us
  waiting for transfers between devices  260 us (51%)
  blocking collectives  108 us (21%)
  local copies, waits for them, and re-layouts  47.8 us (9%)
  matrix products  29.6 us (6%)
  starting transfers between devices  27.5 us (5%)
  other arithmetic  20.6 us (4%)
  between operations  13.7 us (3%)
    all_gather x1, waiting for transfers between devices, body(): value_part = lax.all_gather(value_rows, 'blk', axis=0, tiled=True)  106 us
    all_to_all x1, blocking collectives, body(): lax.all_to_all(partial.reshape(blk_count, block_rows, width), 'blk', 0, 0...  79.4 us
    all_to_all x1, waiting for transfers between devices, body(): lax.all_to_all(jnp.broadcast_to(modin[None], (blk_count,) + modin.shape),...  73.6 us
    all_gather x1, waiting for transfers between devices, body(): key_part = lax.all_gather(key_rot, 'blk', axis=0, tiled=True)  67.6 us
    gather x1, local copies, waits for them, and re-layouts, body(): kept = jnp.take(key_keep, key_ids) == 1  23 us
    all_to_all x1, blocking collectives, body(): lax.all_to_all(lax.all_to_all(attended, 'seq', split_axis=0, concat_axis=...  19.6 us
    all_to_all x1, starting transfers between devices, body(): lax.all_to_all(jnp.broadcast_to(modin[None], (blk_count,) + modin.shape),...  14.3 us
  transfers between devices with their start and end apart: 5, of which 5 were waited for; matrix products, arithmetic and copies ran while one was open for 9% of the time, Pallas kernels for 0%

commit v1 on v0

--- a/solution.py
+++ b/solution.py
@@ -145,7 +145,9 @@
     )
     value_rows = heads4[:, :, 2]
     run_top = jnp.full((query_rows, local_heads), -1e30, jnp.float32)
-    key_part = lax.all_gather(key_rot, "blk", axis=0, tiled=True)
+    key_part = jnp.concatenate(
+        lax.all_to_all(jnp.stack([key_rot] * lax.axis_size("blk")), "blk", 0, 0), axis=0
+    )
     value_part = lax.all_gather(value_rows, "blk", axis=0, tiled=True)
     key_ids = spread_rows(
         jnp.arange(key_part.shape[0], dtype=jnp.int32), query_rows, block_rows, tok_seq

time: 508 us -> 452 us (0.89)
  waiting for transfers between devices: 260 us -> 197 us
  starting transfers between devices: 27.5 us -> 35.5 us
    all_gather x1 -> x0, waiting for transfers between devices: 67.6 us -> none  [body(): key_part = lax.all_gather(key_rot, 'blk', axis=0, tiled=True)]
    all_to_all x0 -> x1, waiting for transfers between devices: none -> 49.2 us  [body(): lax.all_to_all(jnp.stack([key_rot] * lax.axis_size('blk')), 'blk', 0, 0)]
    all_gather x1, waiting for transfers between devices: 106 us -> 61.4 us  [body(): value_part = lax.all_gather(value_rows, 'blk', axis=0, tiled=True)]
    all_to_all x0 -> x1, starting transfers between devices: none -> 8.01 us  [body(): lax.all_to_all(jnp.stack([key_rot] * lax.axis_size('blk')), 'blk', 0, 0)]
  transfers between devices with their start and end apart: 5 -> 5, of which waited for: 5 -> 5; matrix products, arithmetic and copies ran while one was open for 9% -> 10% of each run, Pallas kernels for 0% -> 0%
where the time goes in v1:
time: 452 us; the launch traced here: 451 us
  waiting for transfers between devices  197 us (44%)
  blocking collectives  108 us (24%)
  local copies, waits for them, and re-layouts  51.4 us (11%)
  starting transfers between devices  35.5 us (8%)
  matrix products  27.6 us (6%)
  other arithmetic  18 us (4%)
  between operations  13.7 us (3%)
    all_to_all x1, blocking collectives, body(): lax.all_to_all(partial.reshape(blk_count, block_rows, width), 'blk', 0, 0...  79.4 us
    all_to_all x1, waiting for transfers between devices, body(): lax.all_to_all(jnp.broadcast_to(modin[None], (blk_count,) + modin.shape),...  73.6 us
    all_gather x1, waiting for transfers between devices, body(): value_part = lax.all_gather(value_rows, 'blk', axis=0, tiled=True)  61.4 us
    all_to_all x1, waiting for transfers between devices, body(): lax.all_to_all(jnp.stack([key_rot] * lax.axis_size('blk')), 'blk', 0, 0)  49.2 us
    gather x1, local copies, waits for them, and re-layouts, body(): kept = jnp.take(key_keep, key_ids) == 1  23 us
    all_to_all x1, blocking collectives, body(): lax.all_to_all(lax.all_to_all(attended, 'seq', split_axis=0, concat_axis=...  19.6 us
    all_to_all x1, starting transfers between devices, body(): lax.all_to_all(jnp.broadcast_to(modin[None], (blk_count,) + modin.shape),...  14.3 us
    dot_general x1, matrix products, body(): jnp.dot(mlp_part, w_mlp_out, preferred_element_type=jnp.float32)  9.59 us
  transfers between devices with their start and end apart: 5, of which 5 were waited for; matrix products, arithmetic and copies ran while one was open for 10% of the time, Pallas kernels for 0%

profile of v1, /device:TPU:2, one launch (start us, length us, event | category | flops | bytes accessed | tf_op | source)
XLA Modules:
  0.0 451.0 jit_solution(16291574892750711570)
XLA Ops:
  6.5 0.9 fusion.70
  7.4 1.1 reduce_sum.91
  8.5 1.1 multiply_reduce_fusion.2
  9.6 0.8 reduce-window.8
  10.6 2.8 fusion.11
  13.4 0.4 fusion.44
  13.8 0.1 fusion.41
  14.0 2.0 broadcast_in_dim.66
  16.0 14.3 %all-to-all-start = ((bf16[32,16,3072]{2,1,0:T(8,128)(2,1)}), bf16[32,16,3072]{2,1,0:T(8,128)(2,1)}, u32[]{:S(2)}, u32[]{:S(2)}) async-start(bf16[32,16,3072]{2,1,0:T(8,128)(2,1)} %broadcast_in_dim.66), calls=%async_computation | async-start | bytes 6291456 | tf_op jit(solution)/shard_map/all_to_all | solution.py:113
  30.3 73.6 %all-to-all-done = bf16[32,16,3072]{2,1,0:T(8,128)(2,1)} async-done(((bf16[32,16,3072]{2,1,0:T(8,128)(2,1)}), bf16[32,16,3072]{2,1,0:T(8,128)(2,1)}, u32[]{:S(2)}, u32[]{:S(2)}) %all-to-all-start) | async-done | bytes 3145760 | tf_op jit(solution)/shard_map/all_to_all | solution.py:113
  104.0 3.6 convolution_convert_fusion
  107.5 0.9 copy.81
  108.5 7.2 %all-to-all-start.1 = ((bf16[32,16,288]{2,1,0:T(8,128)(2,1)}), bf16[32,16,288]{2,1,0:T(8,128)(2,1)S(1)}, u32[]{:S(2)}, u32[]{:S(2)}) async-start(bf16[32,16,288]{2,1,0:T(8,128)(2,1)} %bitcast.73), calls=%async_computation.1 | async-start | bytes 786432 | tf_op jit(solution)/shard_map/all_to_all | solution.py:124
  115.7 0.7 mul.314
  116.5 0.7 mul.325
  117.2 2.8 copy.85
  120.0 2.8 gather_fusion.1
  122.9 0.9 copy.86
  123.8 0.5 fusion.78
  124.4 4.0 all-to-all-done.1
  128.4 0.8 copy.82
  129.2 1.5 all_to_all.63
  130.6 0.7 copy.83
  131.4 5.7 %all-to-all-start.2 = ((bf16[16,8,1152]{2,0,1:T(8,128)(2,1)}), bf16[16,8,1152]{2,0,1:T(8,128)(2,1)S(1)}, u32[]{:S(2)}, u32[]{:S(2)}) async-start(bf16[16,8,1152]{2,0,1:T(8,128)(2,1)} %copy.83), calls=%async_computation.2 | async-start | bytes 589824 | tf_op jit(solution)/shard_map/all_to_all | solution.py:123
  137.1 0.7 fusion.71
  137.9 0.8 fusion.87
  138.6 8.9 %all-to-all-done.2 = bf16[16,8,1152]{2,0,1:T(8,128)(2,1)S(1)} async-done(((bf16[16,8,1152]{2,0,1:T(8,128)(2,1)}), bf16[16,8,1152]{2,0,1:T(8,128)(2,1)S(1)}, u32[]{:S(2)}, u32[]{:S(2)}) %all-to-all-start.2) | async-done | bytes 294944 | tf_op jit(solution)/shard_map/all_to_all | solution.py:123
  147.5 0.7 copy-done.5
  148.2 1.0 reshape.633
  149.3 1.1 fusion.86
  150.4 0.2 multiply_reduce_fusion
  150.6 0.7 copy_convert_fusion
  151.3 1.1 copy.88
  152.3 0.8 copy.94
  153.2 0.9 multiply_multiply_fusion.2
  154.0 1.1 multiply_multiply_fusion.1
  155.1 2.0 subtract_convert_fusion
  157.1 0.2 pad_maximum_fusion
  157.3 0.1 copy.91
  157.4 2.5 stack.9
  159.9 8.0 %all-to-all-start.3 = ((bf16[32,128,3,128]{3,1,2,0:T(8,128)(2,1)}), bf16[32,128,3,128]{3,1,2,0:T(8,128)(2,1)}, u32[]{:S(2)}, u32[]{:S(2)}) async-start(bf16[32,128,3,128]{3,1,2,0:T(8,128)(2,1)} %stack.9), calls=%async_computation.3 | async-start | bytes 6291456 | tf_op jit(solution)/shard_map/all_to_all | solution.py:149
  167.9 0.2 all-gather.3.cloned.1.call-start
  168.2 0.8 copy.109
  169.0 0.1 compare_select_fusion
  169.1 23.0 %gather_fusion = s32[4096]{0:T(1024)S(1)} fusion(s32[4096]{0:T(1024)S(1)} %copy-done.1, s32[4096]{0:T(1024)S(1)} %broadcast_clamp_fusion), kind=kCustom, calls=%fused_computation | custom fusion | bytes 49152 | tf_op jit(solution)/shard_map/jit(_take)/gather | solution.py:156
  192.3 0.1 convert_reduce_fusion.1
  192.5 4.5 %or_and_fusion = pred[128,4096]{0,1:T(8,128)(4,1)} fusion(s32[128]{0:T(128)S(1)} %fusion.72, s32[128]{0:T(128)S(1)} %convert_reduce_fusion.2, s32[4096]{0:T(1024)S(1)} %fusion.56, s32[4096]{0:T(1024)S(1)} %convert_reduce_fusion.1, pred[4096]{0:T(1024)(128)(4,1)S(1)} %select_compare_fusion), kind=kLoop, calls=%fused_computation.19 | loop fusion | flops 2097152 | bytes 562176 | tf_op jit(solution)/shard_map/and | solution.py:158
  197.0 0.2 pad_maximum_fusion.1
  197.2 49.2 %all-to-all-done.3 = bf16[32,128,3,128]{3,1,2,0:T(8,128)(2,1)} async-done(((bf16[32,128,3,128]{3,1,2,0:T(8,128)(2,1)}), bf16[32,128,3,128]{3,1,2,0:T(8,128)(2,1)}, u32[]{:S(2)}, u32[]{:S(2)}) %all-to-all-start.3) | async-done | bytes 3145760 | tf_op jit(solution)/shard_map/all_to_all | solution.py:149
  246.4 2.3 copy.92
  248.8 1.2 fusion
  250.0 2.6 copy-done.2
  252.6 1.2 fusion.3
  253.8 61.4 %all-gather.3.cloned.1.call-done = bf16[4096,3,1,128]{0,3,1,2:T(8,128)(2,1)} async-done(((bf16[128,3,1,128]{0,3,1,2:T(8,128)(2,1)}), bf16[4096,3,1,128]{0,3,1,2:T(8,128)(2,1)}) %all-gather.3.cloned.1.call-update) | async-done | bytes 3145744 | tf_op jit(solution)/shard_map/all_gather | solution.py:151
  315.2 5.3 %fusion.23 = bf16[128,3,128]{0,2,1:T(8,128)(2,1)S(1)} fusion(f32[3,4096,128]{2,1,0:T(8,128)} %copy-done.2, f32[128,3]{0,1:T(4,128)S(1)} %broadcast_maximum_fusion, pred[128,4096]{0,1:T(8,128)(4,1)} %or_and_fusion, bf16[4096,3,1,128]{0,3,1,2:T(8,128)(2,1)} %all-gather.3.cloned.1.call-done, f32[128,3]{0,1:T(4,128)S(1)} %fusion.3), kind=kOutput, calls=%fused_computation.24 | convolution fusion | flops 407470080 | bytes 10062848 | tf_op jit(solution)/shard_map/qhk,khd->qhd/dot_general | solution.py:169
  320.5 0.1 copy.99
  320.8 8.7 %all_to_all.82 = bf16[8,16,384]{2,1,0:T(8,128)(2,1)S(1)} all-to-all(bf16[8,16,384]{2,1,0:T(8,128)(2,1)S(1)} %all_to_all.67), channel_id=1, replica_groups=mesh['seq'=8,'blk'=32] {'seq'}, dimensions={0} | all-to-all | bytes 196608 | tf_op jit(solution)/shard_map/all_to_all | solution.py:176
  329.5 0.1 all_to_all.70
  329.7 19.6 %all_to_all.83 = bf16[16,32,96]{2,0,1:T(8,128)(2,1)S(1)} all-to-all(bf16[16,32,96]{2,0,1:T(8,128)(2,1)S(1)} %copy.101), channel_id=1, replica_groups=mesh['seq'=8,'blk'=32] {'blk'}, dimensions={1} | all-to-all | bytes 196608 | tf_op jit(solution)/shard_map/all_to_all | solution.py:175
  349.3 4.7 %fusion.90 = f32[512,3072]{1,0:T(8,128)} fusion(bf16[512,96]{1,0:T(8,128)(2,1)S(1)} %bitcast.75, bf16[96,3072]{1,0:T(8,128)(2,1)} %param.22), kind=kOutput, calls=%fused_computation.169 | convolution fusion | flops 301989888 | bytes 6979584 | tf_op jit(solution)/shard_map/dot_general | solution.py:184
  354.0 9.6 %add_convert_fusion = bf16[512,3072]{1,0:T(8,128)(2,1)} fusion(f32[512,3072]{1,0:T(8,128)} %fusion.90, bf16[384,3072]{1,0:T(8,128)(2,1)S(1)} %copy-done, bf16[512,3072]{1,0:T(8,128)(2,1)} %bitcast.5, bf16[3072,384]{1,0:T(8,128)(2,1)} %param.19), kind=kOutput, calls=%fused_computation.8 | convolution fusion | flops 2420834304 | bytes 17301504 | tf_op jit(solution)/shard_map/dot_general | solution.py:185
  363.6 79.4 %all_to_all.84 = bf16[32,16,3072]{2,1,0:T(8,128)(2,1)S(1)} all-to-all(bf16[32,16,3072]{2,1,0:T(8,128)(2,1)} %bitcast.70), channel_id=1, replica_groups=mesh['seq'=8,'blk'=32] {'blk'}, dimensions={0} | all-to-all | bytes 6291456 | tf_op jit(solution)/shard_map/all_to_all | solution.py:187
  442.9 0.5 convert_reduce_fusion
  443.4 0.7 fusion.43
  (46 shorter events, 0.7 us)
Async XLA Ops:
  6.5 347.4 %copy-start = (bf16[384,3072]{1,0:T(8,128)(2,1)S(1)}, bf16[384,3072]{1,0:T(8,128)(2,1)}, u32[]{:S(2)}) copy-start(bf16[384,3072]{1,0:T(8,128)(2,1)} %param.23) | copy-start | bytes 7077892
  6.5 7.3 %copy-start.3 = (f32[16,3072]{1,0:T(8,128)S(1)}, f32[16,3072]{1,0:T(8,128)}, u32[]{:S(2)}) copy-start(f32[16,3072]{1,0:T(8,128)} %param.12) | copy-start | bytes 589828
  10.5 5.5 %copy-start.11 = (s32[4,1]{0,1:T(1,128)}, s32[4,1]{0,1:T(1,128)S(1)}, u32[]{:S(2)}) copy-start(s32[4,1]{0,1:T(1,128)S(1)} %reduce-window.8) | copy-start | bytes 52
  16.0 87.9 %all-to-all-start = ((bf16[32,16,3072]{2,1,0:T(8,128)(2,1)}), bf16[32,16,3072]{2,1,0:T(8,128)(2,1)}, u32[]{:S(2)}, u32[]{:S(2)}) async-start(bf16[32,16,3072]{2,1,0:T(8,128)(2,1)} %broadcast_in_dim.66), calls=%async_computation | async-start | bytes 6291456 | tf_op jit(solution)/shard_map/all_to_all | solution.py:113
  103.9 11.8 %copy-start.9 = (f32[128]{0:T(128)S(1)}, f32[128]{0:T(128)}, u32[]{:S(2)}) copy-start(f32[128]{0:T(128)} %param.21) | copy-start | bytes 1540
  104.0 12.5 %copy-start.10 = (f32[128]{0:T(128)S(1)}, f32[128]{0:T(128)}, u32[]{:S(2)}) copy-start(f32[128]{0:T(128)} %param.20) | copy-start | bytes 1540
  108.5 19.9 %all-to-all-start.1 = ((bf16[32,16,288]{2,1,0:T(8,128)(2,1)}), bf16[32,16,288]{2,1,0:T(8,128)(2,1)S(1)}, u32[]{:S(2)}, u32[]{:S(2)}) async-start(bf16[32,16,288]{2,1,0:T(8,128)(2,1)} %bitcast.73), calls=%async_computation.1 | async-start | bytes 786432 | tf_op jit(solution)/shard_map/all_to_all | solution.py:124
  131.4 16.2 %all-to-all-start.2 = ((bf16[16,8,1152]{2,0,1:T(8,128)(2,1)}), bf16[16,8,1152]{2,0,1:T(8,128)(2,1)S(1)}, u32[]{:S(2)}, u32[]{:S(2)}) async-start(bf16[16,8,1152]{2,0,1:T(8,128)(2,1)} %copy.83), calls=%async_computation.2 | async-start | bytes 589824 | tf_op jit(solution)/shard_map/all_to_all | solution.py:123
  147.5 0.7 copy-start.5
  159.9 8.2 %copy-start.6 = (bf16[128,3,1,128]{3,2,1,0:T(2,128)(2,1)S(1)}, bf16[128,3,1,128]{3,2,1,0:T(2,128)(2,1)}, u32[]{:S(2)}) copy-start(bf16[128,3,1,128]{3,2,1,0:T(2,128)(2,1)} %get-tuple-element.5) | copy-start | bytes 294916
  159.9 9.2 %copy-start.1 = (s32[4096]{0:T(1024)S(1)}, s32[4096]{0:T(1024)}, u32[]{:S(2)}) copy-start(s32[4096]{0:T(1024)} %param.13) | copy-start | bytes 49156
  159.9 86.5 %all-to-all-start.3 = ((bf16[32,128,3,128]{3,1,2,0:T(8,128)(2,1)}), bf16[32,128,3,128]{3,1,2,0:T(8,128)(2,1)}, u32[]{:S(2)}, u32[]{:S(2)}) async-start(bf16[32,128,3,128]{3,1,2,0:T(8,128)(2,1)} %stack.9), calls=%async_computation.3 | async-start | bytes 6291456 | tf_op jit(solution)/shard_map/all_to_all | solution.py:149
  167.9 147.2 %all-gather.3.cloned.1.call-start = ((), (), s32[]{:S(2)}) async-start(), calls=%async_computation.7 | async-start | bytes 3244032 | tf_op jit(solution)/shard_map/all_gather | solution.py:151
  169.1 23.1 %copy-start.12 = (s32[4,1]{0,1:T(1,128)S(1)}, s32[4,1]{0,1:T(1,128)}, u32[]{:S(2)}) copy-start(s32[4,1]{0,1:T(1,128)} %copy-done.11) | copy-start | bytes 52
  169.1 27.9 %copy-start.7 = (bf16[128,3,64,1]{0,3,2,1:T(2,128)(2,1)S(1)}, bf16[128,3,64,1]{0,3,2,1:T(2,128)(2,1)}, u32[]{:S(2)}) copy-start(bf16[128,3,64,1]{0,3,2,1:T(2,128)(2,1)} %get-tuple-element.8) | copy-start | bytes 147460
  169.1 27.9 %copy-start.8 = (bf16[128,3,64,1]{0,3,2,1:T(2,128)(2,1)S(1)}, bf16[128,3,64,1]{0,3,2,1:T(2,128)(2,1)}, u32[]{:S(2)}) copy-start(bf16[128,3,64,1]{0,3,2,1:T(2,128)(2,1)} %get-tuple-element.9) | copy-start | bytes 147460
  246.4 2.4 copy-start.4
  250.0 2.7 copy-start.2
Sparse Core Ops, SparseCore 0:
  172.0 143.1 all-gather.2
